TPU v7x, 256 devices: a whole 4x4x8 slice. The times are simulated.
256 devices in a mesh: elem: 32 (over z, x), blk: 8 (over y, core).
Axes of the slice: x: 4, y: 4, z: 8, core: 2. Of those that a mesh axis runs over, the one named last changes fastest.
Arguments:
- basis: bfloat16 [32768, 3, 512], P('elem'), may hold values from -6 to 6
- send_rows: int32 [32, 8, 256], P('elem', 'blk'), may hold values from 0 to 1023
- elem_slot: int32 [8, 16384], P(None, ('elem', 'blk')), may hold values from 0 to 255, as said below
- set_size: int32 [32], replicated, may hold values from 1 to 512, 10240 in all
- elem_weight: float32 [16384], P(('elem', 'blk')), may hold values from 0.2 to 5
- element_stiffening: float32 [16384], P(('elem', 'blk')), may hold values from 1 to 8
- state: bfloat16 [512], replicated, may hold values from -0.25 to 0.25
- load: float32 [512], P('blk'), may hold values from -6 to 6
Outputs:
- tangent: float32 [512, 512], P('elem', 'blk')
- residual: float32 [512], P('blk')
Inputs may be any that keep to these rules, and one draw needn't show every extreme that they name: `elem_slot`: for element column of device (s, b): p names slot p % 8 of what owner p // 8 sends to that device. From each owner only its first n slots are named, n at most 8; for every device exactly one owner gives 8, and the n over all owners sum to 128.
All inputs are finite; a program needn't handle non-finite values.
Results may differ from a plain program's by a relative error of at most 0.0003.
Values may be sent and summed in bfloat16 or wider, within the bound.
No kernel may reach another device: no remote copies, remote signals or barrier semaphores. Data moves between devices by JAX's collectives and lax.ppermute only.
A program may use at most 64 MiB of HBM per device.

v0:
```python
import jax
import jax.numpy as jnp
from jax import lax
from jax.sharding import PartitionSpec as P


def corner_grads():
    corner = jnp.arange(8)[:, None]
    bit = corner // 2 ** jnp.arange(3)[None, :] % 2
    return (bit * 2 - 1).astype(jnp.float32) * 0.25


def element_contributions(basis_matrix, displacement, stiffening_power):
    grads = corner_grads()
    element_count = basis_matrix.shape[0]
    basis_modes = basis_matrix.shape[2]
    corner_nodes = basis_matrix.reshape(element_count, 8, 3, basis_modes)
    grad_basis = jnp.einsum(
        "ak,eacm->ekcm",
        grads.astype(jnp.bfloat16),
        corner_nodes,
        preferred_element_type=jnp.float32,
    )
    moved = displacement.reshape(8, 3, element_count)
    hgrad = jnp.einsum("ak,ace->kce", grads, moved, precision=lax.Precision.HIGHEST)
    volume = hgrad[0, 0] + hgrad[1, 1] + hgrad[2, 2]
    stiff = 1.0 + stiffening_power * volume**2 - 2.0 / 3.0
    press = volume + stiffening_power * volume**3 / 3.0 - 2.0 / 3.0 * volume
    eye = jnp.eye(3, dtype=jnp.float32)
    stress = hgrad + jnp.transpose(hgrad, (1, 0, 2)) + press[None, None, :] * eye[:, :, None]
    force_vector = (
        jnp.einsum("ak,kce->ace", grads, stress, precision=lax.Precision.HIGHEST).reshape(
            24, element_count
        )
        + 0.25 * displacement
    )
    sym = grad_basis + jnp.transpose(grad_basis, (0, 2, 1, 3))
    trace_basis = grad_basis[:, 0, 0] + grad_basis[:, 1, 1] + grad_basis[:, 2, 2]
    mode_image = jnp.einsum("ak,ekcm->eacm", grads, sym, precision=lax.Precision.HIGHEST)
    mode_image = (
        mode_image
        + stiff[:, None, None, None] * grads[None, :, :, None] * trace_basis[:, None, None, :]
        + 0.25 * corner_nodes.astype(jnp.float32)
    )
    return (mode_image.reshape(element_count, 24, basis_modes), force_vector)


def local(basis, send_rows, elem_slot, set_size, elem_weight, element_stiffening, state, load):
    nodes = basis.shape[0]
    basis_modes = basis.shape[2]
    n_elem = lax.psum(1, "elem")
    n_blk = lax.psum(1, "blk")
    flat = basis.reshape(nodes, 3 * basis_modes)
    outgoing = jnp.take(flat, send_rows[0, 0], axis=0)
    arrived = lax.all_to_all(outgoing, "elem", split_axis=0, concat_axis=0, tiled=True)
    element_count = elem_slot.shape[1]
    chosen_elements = jnp.take(arrived, elem_slot.T.reshape(-1), axis=0)
    basis_matrix = chosen_elements.reshape(element_count, 24, basis_modes)
    set_index = lax.axis_index("elem")
    block_index = lax.axis_index("blk")
    live = lax.dynamic_index_in_dim(set_size, set_index, keepdims=False)
    position = block_index * element_count + jnp.arange(element_count, dtype=jnp.int32)
    weights = jnp.where(position < live, elem_weight, jnp.zeros_like(elem_weight))
    displacement = jnp.einsum("agd,d->ga", basis_matrix, state, preferred_element_type=jnp.float32)
    mode_image, force_vector = element_contributions(basis_matrix, displacement, element_stiffening)
    weighted_image = (weights[:, None, None] * mode_image).astype(jnp.bfloat16)
    weighted_force = (force_vector * weights[None, :]).astype(jnp.bfloat16)
    rows = basis_modes // n_elem
    cols = basis_modes // n_blk
    tangent = lax.dot_general(
        basis_matrix,
        weighted_image,
        (((0, 1), (0, 1)), ((), ())),
        preferred_element_type=jnp.float32,
    )
    force_all = lax.dot_general(
        basis_matrix,
        weighted_force,
        (((0, 1), (1, 0)), ((), ())),
        preferred_element_type=jnp.float32,
    )
    pad = jnp.zeros((7, basis_modes), jnp.float32)
    stacked = jnp.concatenate([tangent, force_all[None, :], pad], axis=0)
    parts = lax.all_to_all(stacked, "blk", split_axis=1, concat_axis=0, tiled=True)
    halfway = jnp.sum(parts.reshape(n_blk, basis_modes + 8, cols), axis=0)
    force_cols = halfway[basis_modes]
    tangent_rows = halfway[:basis_modes].reshape(n_elem, rows, cols)
    chunks = jnp.concatenate(
        [tangent_rows, jnp.broadcast_to(force_cols[None, None, :], (n_elem, 1, cols))], axis=1
    )
    arrived_chunks = lax.all_to_all(chunks, "elem", split_axis=0, concat_axis=0, tiled=True)
    mine = jnp.sum(arrived_chunks, axis=0)
    scale = lax.rsqrt(24.0 * jnp.sum(set_size).astype(jnp.float32))
    return (mine[:rows] * scale, mine[rows] * scale - load)


def solution(mesh):
    in_specs = (
        P("elem", None, None),
        P("elem", "blk", None),
        P(None, ("elem", "blk")),
        P(),
        P(("elem", "blk")),
        P(("elem", "blk")),
        P(),
        P("blk"),
    )
    out_specs = (P("elem", "blk"), P("blk"))
    return jax.shard_map(local, mesh=mesh, in_specs=in_specs, out_specs=out_specs, check_vma=False)
```

profile of v0, /device:TPU:1, one launch (start us, length us, event | category | flops | bytes accessed | tf_op | source)
XLA Modules:
  0.0 132.4 jit_solution(6316363443217147849)
XLA Ops:
  0.6 4.7 %copy.47 = bf16[1024,3,512]{0,2,1:T(8,128)(2,1)} copy(bf16[1024,3,512]{2,0,1:T(8,128)(2,1)} %param.8) | data formatting | bytes 6291456 | tf_op args[0]
  5.3 3.2 %copy.48 = bf16[1024,1536]{1,0:T(8,128)(2,1)S(1)} copy(bf16[1024,1536]{0,1:T(8,128)(2,1)} %bitcast.91) | data formatting | bytes 6291456 | tf_op jit(solution)/shard_map/reshape | solution.py:53
  9.8 2.1 %gather_fusion = bf16[256,1536]{1,0:T(8,128)(2,1)} fusion(bf16[1024,1536]{1,0:T(8,128)(2,1)S(1)} %copy.48, s32[1024]{0:T(1024)S(1)} %pad_clamp_fusion.1), kind=kCustom, calls=%fused_computation | custom fusion | bytes 1573888 | tf_op jit(solution)/shard_map/jit(_take)/gather | solution.py:54
  12.0 2.2 %bitcast_select_fusion = bf16[32,8,1536]{2,1,0:T(8,128)(2,1)} fusion(bf16[256,1536]{1,0:T(8,128)(2,1)} %gather_fusion, pred[32,8]{1,0:T(8,128)(4,1)S(1)} %compare_and_fusion), kind=kLoop, calls=%fused_computation.21 | loop fusion | flops 393216 | bytes 1573120 | tf_op jit(solution)/shard_map/jit(_take)/select_n | solution.py:54
  14.2 11.9 %all-to-all-start = ((bf16[32,8,1536]{2,1,0:T(8,128)(2,1)}), bf16[32,8,1536]{2,1,0:T(8,128)(2,1)S(1)}, u32[]{:S(2)}, u32[]{:S(2)}) async-start(bf16[32,8,1536]{2,1,0:T(8,128)(2,1)} %bitcast_select_fusion), calls=%async_computation | async-start | bytes 1572864 | tf_op jit(solution)/shard_map/all_to_all | solution.py:55
  29.3 17.8 %all-to-all-done = bf16[32,8,1536]{2,1,0:T(8,128)(2,1)S(1)} async-done(((bf16[32,8,1536]{2,1,0:T(8,128)(2,1)}), bf16[32,8,1536]{2,1,0:T(8,128)(2,1)S(1)}, u32[]{:S(2)}, u32[]{:S(2)}) %all-to-all-start) | async-done | bytes 786464 | tf_op jit(solution)/shard_map/all_to_all | solution.py:55
  47.1 2.1 %gather_fusion.1 = bf16[512,1536]{1,0:T(8,128)(2,1)S(1)} fusion(bf16[256,1536]{1,0:T(8,128)(2,1)S(1)} %bitcast.88, s32[1024]{0:T(1024)S(1)} %pad_clamp_fusion), kind=kCustom, calls=%fused_computation.1 | custom fusion | bytes 3147776 | tf_op jit(solution)/shard_map/jit(_take)/gather | solution.py:57
  49.3 1.6 %gather.18 = bf16[64,24,512]{2,1,0:T(8,128)(2,1)} reshape(bf16[512,1536]{1,0:T(8,128)(2,1)S(1)} %gather_fusion.1) | data formatting | bytes 3145728 | tf_op jit(solution)/shard_map/jit(_take)/gather | solution.py:57
  51.7 1.8 %copy.93 = f32[64,3,512,3]{2,1,3,0:T(4,128)} copy(f32[64,3,512,3]{2,3,1,0:T(4,128)S(1)} %fusion.10) | data formatting | bytes 2359296 | tf_op jit(solution)/shard_map/ak,eacm->ekcm/dot_general | solution.py:18
  53.5 2.0 %bitcast_add_fusion.1 = f32[64,3,3,512]{3,2,1,0:T(4,128)} fusion(f32[64,3,512,3]{2,3,1,0:T(4,128)S(1)} %fusion.10), kind=kLoop, calls=%fused_computation.10 | loop fusion | flops 294912 | bytes 2359296 | tf_op jit(solution)/shard_map/add | solution.py:37
  55.4 1.4 %fusion.8 = bf16[512,64,24]{0,2,1:T(8,128)(2,1)} fusion(bf16[64,24,512]{2,1,0:T(8,128)(2,1)S(1)} %copy-done, pred[64,24]{1,0:T(8,128)(4,1)S(1)} %copy.46), kind=kLoop, calls=%fused_computation.15 | loop fusion | flops 786432 | bytes 3147264 | tf_op jit(solution)/shard_map/dot_general | solution.py:76
  56.8 1.5 %fusion.9 = f32[1,64,24]{2,0,1:T(1,128)S(1)} fusion(bf16[512,1,1]{0,1,2:T(2,128)(2,1)S(1)} %reshape.343, bf16[64,24,512]{2,1,0:T(8,128)(2,1)S(1)} %copy-done, pred[64,24]{1,0:T(8,128)(4,1)S(1)} %copy.46), kind=kOutput, calls=%fused_computation.16 | convolution fusion | flops 2359296 | bytes 1581568 | tf_op jit(solution)/shard_map/agd,d->ga/dot_general | solution.py:64
  58.8 1.7 %slice_add_fusion = f32[64,1,1,512]{3,2,1,0:T(1,128)S(1)} fusion(f32[64,3,3,512]{3,2,1,0:T(4,128)} %bitcast.93), kind=kLoop, calls=%fused_computation.26 | loop fusion | flops 65536 | bytes 524288 | tf_op jit(solution)/shard_map/add | solution.py:38
  60.6 5.7 %fusion.4 = bf16[64,8,3,512]{3,1,2,0:T(8,128)(2,1)S(1)} fusion(f32[64,3,3,512]{3,2,1,0:T(4,128)} %bitcast_add_fusion.1, f32[64,512]{1,0:T(8,128)S(1)} %bitcast.95, f32[64,8,3]{1,2,0:T(4,128)S(1)} %broadcast_multiply_fusion, f32[64]{0:T(128)S(1)} %compare_select_fusion.10, bf16[64,8,3,512]{3,1,2,0:T(8,128)(2,1)S(1)} %bitcast.90, pred[64,8]{1,0:T(8,128)(4,1)S(1)} %copy.50, ...), kind=kOutput, calls=%fused_computation.7 | convolution fusion | flops 34603536 | bytes 4463416 | tf_op jit(solution)/shard_map/ak,ekcm->eacm/dot_general | solution.py:39
  66.3 1.7 %copy.54 = bf16[64,8,3,512]{3,0,2,1:T(8,128)(2,1)} copy(bf16[64,8,3,512]{3,1,2,0:T(8,128)(2,1)S(1)} %fusion.4) | data formatting | bytes 3145728 | tf_op jit(solution)/shard_map/convert_element_type | solution.py:66
  68.0 5.1 %reshape.350 = bf16[8,64,64,24]{1,0,2,3:T(8,128)(2,1)} reshape(bf16[512,64,24]{0,1,2:T(8,128)(2,1)} %bitcast.92) | data formatting | bytes 3145728 | tf_op jit(solution)/shard_map/dot_general | solution.py:70
  73.1 1.4 %broadcast_select_fusion.4 = bf16[512,1536]{1,0:T(8,128)(2,1)} fusion(pred[512,1536]{1,0:T(8,128)(4,1)S(1)} %broadcast_in_dim.62, bf16[512,1536]{1,0:T(8,128)(2,1)S(1)} %gather_fusion.1), kind=kLoop, calls=%fused_computation.24 | loop fusion | flops 786432 | bytes 3932160 | tf_op jit(solution)/shard_map/jit(_take)/select_n | solution.py:57
  74.5 2.7 %reshape.346 = bf16[64,24,512,1]{2,1,0,3:T(8,128)(2,1)S(1)} reshape(bf16[512,1536]{1,0:T(8,128)(2,1)} %broadcast_select_fusion.4) | data formatting | bytes 3145728 | tf_op jit(solution)/shard_map/jit(_take)/select_n | solution.py:57
  77.7 3.0 %reshape.322 = bf16[8,64,64,24]{1,0,3,2:T(8,128)(2,1)} reshape(bf16[512,64,24]{0,2,1:T(8,128)(2,1)S(1)} %copy-done.1) | data formatting | bytes 3145728 | tf_op jit(solution)/shard_map/reshape.256
  80.8 4.5 %fusion.11 = f32[512,8,64]{0,2,1:T(8,128)S(1)} fusion(bf16[64,24,512,1]{2,1,0,3:T(8,128)(2,1)S(1)} %reshape.346, bf16[8,64,64,24]{1,0,2,3:T(8,128)(2,1)} %reshape.350), kind=kOutput, calls=%fused_computation.18 | convolution fusion | flops 805306368 | bytes 4194304 | tf_op jit(solution)/shard_map/dot_general | solution.py:70
  85.3 3.6 %fusion.14 = f32[1,8,64]{0,2,1:T(8,128)S(1)} fusion(bf16[8,64,64,24]{1,0,3,2:T(8,128)(2,1)S(1)} %copy-done.2, bf16[24,64,1,1]{1,0,2,3:T(8,128)(2,1)S(1)} %fusion.22), kind=kOutput, calls=%fused_computation.20 | convolution fusion | flops 1572864 | bytes 1577984 | tf_op jit(solution)/shard_map/dot_general | solution.py:76
  89.1 25.0 %all_to_all.24 = f32[520,8,64]{0,2,1:T(8,128)S(1)} all-to-all(f32[520,8,64]{0,2,1:T(8,128)S(1)} %maximum_maximum_fusion), channel_id=1, replica_groups=mesh['elem'=32,'blk'=8] {'blk'}, dimensions={1} | all-to-all | bytes 2129920 | tf_op jit(solution)/shard_map/all_to_all | solution.py:84
  115.4 4.8 %all-to-all-start.2 = ((f32[32,1,1088]{2,1,0:T(1,128)}), f32[32,1,1088]{2,1,0:T(1,128)S(1)}, u32[]{:S(2)}, u32[]{:S(2)}) async-start(f32[32,1,1088]{2,1,0:T(1,128)} %reshape.362), calls=%async_computation.2 | async-start | bytes 294912 | tf_op jit(solution)/shard_map/all_to_all | solution.py:91
  121.5 8.2 %all-to-all-done.2 = f32[32,1,1088]{2,1,0:T(1,128)S(1)} async-done(((f32[32,1,1088]{2,1,0:T(1,128)}), f32[32,1,1088]{2,1,0:T(1,128)S(1)}, u32[]{:S(2)}, u32[]{:S(2)}) %all-to-all-start.2) | async-done | bytes 139296 | tf_op jit(solution)/shard_map/all_to_all | solution.py:91
  (73 shorter events, 11.0 us)
Async XLA Ops:
  5.3 3.2 %copy-start.4 = (s32[1,1,256]{2,1,0:T(1,128)S(1)}, s32[1,1,256]{2,1,0:T(1,128)}, u32[]{:S(2)}) copy-start(s32[1,1,256]{2,1,0:T(1,128)} %param.9) | copy-start | bytes 3076
  12.0 14.1 %copy-start.3 = (s32[8,64]{1,0:T(8,128)S(1)}, s32[8,64]{1,0:T(8,128)}, u32[]{:S(2)}) copy-start(s32[8,64]{1,0:T(8,128)} %param.10) | copy-start | bytes 6148
  12.0 14.6 %copy-start.5 = (bf16[512]{0:T(512)(128)(2,1)S(1)}, bf16[512]{0:T(512)(128)(2,1)}, u32[]{:S(2)}) copy-start(bf16[512]{0:T(512)(128)(2,1)} %param.14) | copy-start | bytes 3076
  14.2 32.9 %all-to-all-start = ((bf16[32,8,1536]{2,1,0:T(8,128)(2,1)}), bf16[32,8,1536]{2,1,0:T(8,128)(2,1)S(1)}, u32[]{:S(2)}, u32[]{:S(2)}) async-start(bf16[32,8,1536]{2,1,0:T(8,128)(2,1)} %bitcast_select_fusion), calls=%async_computation | async-start | bytes 1572864 | tf_op jit(solution)/shard_map/all_to_all | solution.py:55
  26.1 1.6 %copy-start.9 = (s32[32]{0:T(128)S(1)}, s32[32]{0:T(128)}, u32[]{:S(2)}) copy-start(s32[32]{0:T(128)} %param.11) | copy-start | bytes 388
  26.1 2.4 %copy-start.6 = (f32[64]{0:T(128)S(1)}, f32[64]{0:T(128)}, u32[]{:S(2)}) copy-start(f32[64]{0:T(128)} %param.12) | copy-start | bytes 772
  53.5 2.0 %copy-start = (bf16[64,24,512]{2,1,0:T(8,128)(2,1)S(1)}, bf16[64,24,512]{2,1,0:T(8,128)(2,1)}, u32[]{:S(2)}) copy-start(bf16[64,24,512]{2,1,0:T(8,128)(2,1)} %gather.18) | copy-start | bytes 4718596
  56.8 3.6 %copy-start.7 = (f32[64]{0:T(128)S(1)}, f32[64]{0:T(128)}, u32[]{:S(2)}) copy-start(f32[64]{0:T(128)} %param.13) | copy-start | bytes 772
  74.5 3.2 %copy-start.1 = (bf16[512,64,24]{0,2,1:T(8,128)(2,1)S(1)}, bf16[512,64,24]{0,2,1:T(8,128)(2,1)}, u32[]{:S(2)}) copy-start(bf16[512,64,24]{0,2,1:T(8,128)(2,1)} %fusion.8) | copy-start | bytes 4718596
  80.8 4.5 %copy-start.2 = (bf16[8,64,64,24]{1,0,3,2:T(8,128)(2,1)S(1)}, bf16[8,64,64,24]{1,0,3,2:T(8,128)(2,1)}, u32[]{:S(2)}) copy-start(bf16[8,64,64,24]{1,0,3,2:T(8,128)(2,1)} %reshape.322) | copy-start | bytes 4718596
  114.3 17.6 %copy-start.8 = (f32[64]{0:T(128)S(1)}, f32[64]{0:T(128)}, u32[]{:S(2)}) copy-start(f32[64]{0:T(128)} %param.15) | copy-start | bytes 772
  115.4 14.3 %all-to-all-start.2 = ((f32[32,1,1088]{2,1,0:T(1,128)}), f32[32,1,1088]{2,1,0:T(1,128)S(1)}, u32[]{:S(2)}, u32[]{:S(2)}) async-start(f32[32,1,1088]{2,1,0:T(1,128)} %reshape.362), calls=%async_computation.2 | async-start | bytes 294912 | tf_op jit(solution)/shard_map/all_to_all | solution.py:91
where the time goes:
time: 133 us; the launch traced here: 132 us
  local copies, waits for them, and re-layouts  32.8 us (25%)
  waiting for transfers between devices  26 us (20%)
  blocking collectives  25 us (19%)
  matrix products  16.9 us (13%)
  starting transfers between devices  16.7 us (13%)
  other arithmetic  13.4 us (10%)
  between operations  1.7 us (1%)
    all_to_all x1, blocking collectives, local(): lax.all_to_all(stacked, 'blk', split_axis=1, concat_axis=0, tiled=True)  25 us
    all_to_all x1, waiting for transfers between devices, local(): lax.all_to_all(outgoing, 'elem', split_axis=0, concat_axis=0, tiled=True)  17.8 us
    all_to_all x1, starting transfers between devices, local(): lax.all_to_all(outgoing, 'elem', split_axis=0, concat_axis=0, tiled=True)  11.9 us
    all_to_all x1, waiting for transfers between devices, local(): lax.all_to_all(chunks, 'elem', split_axis=0, concat_axis=0, tiled=True)  8.16 us
    unnamed x26, local copies, waits for them, and re-layouts  6.21 us
    dot_general x1, matrix products, element_contributions(): jnp.einsum('ak,ekcm->eacm', grads, sym, precision=lax.Precision.HIGHEST)  5.69 us
    dot_general x1, local copies, waits for them, and re-layouts, local(): lax.dot_general(basis_matrix, weighted_image, (((0, 1), (0, 1)), ((), ())...  5.14 us
    all_to_all x1, starting transfers between devices, local(): lax.all_to_all(chunks, 'elem', split_axis=0, concat_axis=0, tiled=True)  4.79 us
  transfers between devices with their start and end apart: 2, of which 2 were waited for; matrix products, arithmetic and copies ran while one was open for 3% of the time, Pallas kernels for 0%

commit v1 on v0

--- a/solution.py
+++ b/solution.py
@@ -81,7 +81,10 @@
     )
     pad = jnp.zeros((7, basis_modes), jnp.float32)
     stacked = jnp.concatenate([tangent, force_all[None, :], pad], axis=0)
-    parts = lax.all_to_all(stacked, "blk", split_axis=1, concat_axis=0, tiled=True)
+    parts = jnp.concatenate(
+        lax.all_to_all(jnp.stack(jnp.split(stacked, lax.axis_size("blk"), axis=1)), "blk", 0, 0),
+        axis=0,
+    )
     halfway = jnp.sum(parts.reshape(n_blk, basis_modes + 8, cols), axis=0)
     force_cols = halfway[basis_modes]
     tangent_rows = halfway[:basis_modes].reshape(n_elem, rows, cols)

time: 133 us -> 122 us (0.917)
  matrix products: 16.9 us -> 11.7 us
  local copies, waits for them, and re-layouts: 32.8 us -> 28.3 us
  other arithmetic: 13.4 us -> 11.9 us
    dot_general x1 -> x0, local copies, waits for them, and re-layouts: 5.14 us -> none  [local(): lax.dot_general(basis_matrix, weighted_image, (((0, 1), (0, 1)), ((), ())...]
    dot_general x1, matrix products: 3.62 us -> 0.44 us  [local(): lax.dot_general(basis_matrix, weighted_force, (((0, 1), (1, 0)), ((), ())...]
    another operation x1 -> x2, local copies, waits for them, and re-layouts: 3.04 us -> 1.09 us  [local(): jnp.stack(jnp.split(stacked, lax.axis_size('blk'), axis=1))]
    dot_general x1, matrix products: 4.54 us -> 2.65 us  [local(): lax.dot_general(basis_matrix, weighted_image, (((0, 1), (0, 1)), ((), ())...]
    dot_general x1 -> x0, other arithmetic: 1.41 us -> none  [local(): lax.dot_general(basis_matrix, weighted_force, (((0, 1), (1, 0)), ((), ())...]
    unnamed x26 -> x33, local copies, waits for them, and re-layouts: 6.21 us -> 7.55 us
where the time goes in v1:
time: 122 us; the launch traced here: 121 us
  local copies, waits for them, and re-layouts  28.3 us (23%)
  waiting for transfers between devices  26 us (21%)
  blocking collectives  25 us (20%)
  starting transfers between devices  16.7 us (14%)
  other arithmetic  11.9 us (10%)
  matrix products  11.7 us (10%)
  between operations  1.76 us (1%)
    all_to_all x1, blocking collectives, local(): lax.all_to_all(jnp.stack(jnp.split(stacked, lax.axis_size('blk'), axis=1)...  25 us
    all_to_all x1, waiting for transfers between devices, local(): lax.all_to_all(outgoing, 'elem', split_axis=0, concat_axis=0, tiled=True)  17.8 us
    all_to_all x1, starting transfers between devices, local(): lax.all_to_all(outgoing, 'elem', split_axis=0, concat_axis=0, tiled=True)  11.9 us
    all_to_all x1, waiting for transfers between devices, local(): lax.all_to_all(chunks, 'elem', split_axis=0, concat_axis=0, tiled=True)  8.16 us
    unnamed x33, local copies, waits for them, and re-layouts  7.55 us
    dot_general x1, matrix products, element_contributions(): jnp.einsum('ak,ekcm->eacm', grads, sym, precision=lax.Precision.HIGHEST)  5.61 us
    all_to_all x1, starting transfers between devices, local(): lax.all_to_all(chunks, 'elem', split_axis=0, concat_axis=0, tiled=True)  4.8 us
    select_n x1, local copies, waits for them, and re-layouts, local(): chosen_elements = jnp.take(arrived, elem_slot.T.reshape(-1), axis=0)  3.81 us
  transfers between devices with their start and end apart: 2, of which 2 were waited for; matrix products, arithmetic and copies ran while one was open for 3% of the time, Pallas kernels for 0%

profile of v1, /device:TPU:1, one launch (start us, length us, event | category | flops | bytes accessed | tf_op | source)
XLA Modules:
  0.0 121.3 jit_solution(9407260219563906919)
XLA Ops:
  0.6 4.7 %copy.56 = bf16[1024,3,512]{0,2,1:T(8,128)(2,1)} copy(bf16[1024,3,512]{2,0,1:T(8,128)(2,1)} %param.8) | data formatting | bytes 6291456 | tf_op args[0]
  5.3 3.2 %copy.57 = bf16[1024,1536]{1,0:T(8,128)(2,1)S(1)} copy(bf16[1024,1536]{0,1:T(8,128)(2,1)} %bitcast.111) | data formatting | bytes 6291456 | tf_op jit(solution)/shard_map/reshape | solution.py:53
  9.8 2.1 %gather_fusion = bf16[256,1536]{1,0:T(8,128)(2,1)} fusion(bf16[1024,1536]{1,0:T(8,128)(2,1)S(1)} %copy.57, s32[1024]{0:T(1024)S(1)} %pad_clamp_fusion.1), kind=kCustom, calls=%fused_computation | custom fusion | bytes 1573888 | tf_op jit(solution)/shard_map/jit(_take)/gather | solution.py:54
  12.0 2.2 %bitcast_select_fusion = bf16[32,8,1536]{2,1,0:T(8,128)(2,1)} fusion(bf16[256,1536]{1,0:T(8,128)(2,1)} %gather_fusion, pred[32,8]{1,0:T(8,128)(4,1)S(1)} %compare_and_fusion), kind=kLoop, calls=%fused_computation.19 | loop fusion | flops 393216 | bytes 1573120 | tf_op jit(solution)/shard_map/jit(_take)/select_n | solution.py:54
  14.2 11.9 %all-to-all-start = ((bf16[32,8,1536]{2,1,0:T(8,128)(2,1)}), bf16[32,8,1536]{2,1,0:T(8,128)(2,1)S(1)}, u32[]{:S(2)}, u32[]{:S(2)}) async-start(bf16[32,8,1536]{2,1,0:T(8,128)(2,1)} %bitcast_select_fusion), calls=%async_computation | async-start | bytes 1572864 | tf_op jit(solution)/shard_map/all_to_all | solution.py:55
  26.8 0.9 broadcast_in_dim.64
  29.3 17.8 %all-to-all-done = bf16[32,8,1536]{2,1,0:T(8,128)(2,1)S(1)} async-done(((bf16[32,8,1536]{2,1,0:T(8,128)(2,1)}), bf16[32,8,1536]{2,1,0:T(8,128)(2,1)S(1)}, u32[]{:S(2)}, u32[]{:S(2)}) %all-to-all-start) | async-done | bytes 786464 | tf_op jit(solution)/shard_map/all_to_all | solution.py:55
  47.1 2.1 %gather_fusion.1 = bf16[512,1536]{1,0:T(8,128)(2,1)S(1)} fusion(bf16[256,1536]{1,0:T(8,128)(2,1)S(1)} %bitcast.108, s32[1024]{0:T(1024)S(1)} %pad_clamp_fusion), kind=kCustom, calls=%fused_computation.1 | custom fusion | bytes 3147776 | tf_op jit(solution)/shard_map/jit(_take)/gather | solution.py:57
  49.3 1.7 %gather.18 = bf16[64,24,512]{2,1,0:T(8,128)(2,1)} reshape(bf16[512,1536]{1,0:T(8,128)(2,1)S(1)} %gather_fusion.1) | data formatting | bytes 3145728 | tf_op jit(solution)/shard_map/jit(_take)/gather | solution.py:57
  51.7 1.8 %copy.90 = f32[64,3,512,3]{2,1,3,0:T(4,128)} copy(f32[64,3,512,3]{2,3,1,0:T(4,128)S(1)} %fusion.8) | data formatting | bytes 2359296 | tf_op jit(solution)/shard_map/ak,eacm->ekcm/dot_general | solution.py:18
  53.5 1.9 %bitcast_add_fusion.1 = f32[64,3,3,512]{3,2,1,0:T(4,128)} fusion(f32[64,3,512,3]{2,3,1,0:T(4,128)S(1)} %fusion.8), kind=kLoop, calls=%fused_computation.6 | loop fusion | flops 294912 | bytes 2359296 | tf_op jit(solution)/shard_map/add | solution.py:37
  55.4 1.5 %fusion.7 = f32[1,64,24]{2,0,1:T(1,128)S(1)} fusion(bf16[512,1,1]{0,1,2:T(2,128)(2,1)S(1)} %reshape.326, bf16[64,24,512]{2,1,0:T(8,128)(2,1)S(1)} %copy-done, pred[64,24]{1,0:T(8,128)(4,1)S(1)} %copy.55), kind=kOutput, calls=%fused_computation.14 | convolution fusion | flops 2359296 | bytes 1581568 | tf_op jit(solution)/shard_map/agd,d->ga/dot_general | solution.py:64
  57.4 1.7 %slice_add_fusion = f32[64,1,1,512]{3,2,1,0:T(1,128)S(1)} fusion(f32[64,3,3,512]{3,2,1,0:T(4,128)} %bitcast.112), kind=kLoop, calls=%fused_computation.41 | loop fusion | flops 65536 | bytes 524288 | tf_op jit(solution)/shard_map/add | solution.py:38
  59.2 5.6 %fusion.2 = bf16[64,8,3,512]{3,1,2,0:T(8,128)(2,1)S(1)} fusion(f32[64,3,3,512]{3,2,1,0:T(4,128)} %bitcast_add_fusion.1, f32[64,512]{1,0:T(8,128)S(1)} %bitcast.115, f32[64,8,3]{1,2,0:T(4,128)S(1)} %broadcast_multiply_fusion, f32[64]{0:T(128)S(1)} %compare_select_fusion.10, bf16[64,8,3,512]{3,1,2,0:T(8,128)(2,1)S(1)} %bitcast.110, ...), kind=kOutput, calls=%fused_computation.5 | convolution fusion | flops 34603536 | bytes 4463416 | tf_op jit(solution)/shard_map/ak,ekcm->eacm/dot_general | solution.py:39
  64.8 1.7 %copy.63 = bf16[64,8,3,512]{3,0,2,1:T(8,128)(2,1)} copy(bf16[64,8,3,512]{3,1,2,0:T(8,128)(2,1)S(1)} %fusion.2) | data formatting | bytes 3145728 | tf_op jit(solution)/shard_map/convert_element_type | solution.py:66
  66.5 1.4 %broadcast_select_fusion.7 = bf16[512,1536]{1,0:T(8,128)(2,1)} fusion(pred[512,1536]{1,0:T(8,128)(4,1)S(1)} %broadcast_in_dim.64, bf16[512,1536]{1,0:T(8,128)(2,1)S(1)} %gather_fusion.1), kind=kLoop, calls=%fused_computation.23 | loop fusion | flops 786432 | bytes 3932160 | tf_op jit(solution)/shard_map/jit(_take)/select_n | solution.py:57
  67.9 3.8 %select_n.226 = bf16[64,24,512]{2,1,0:T(8,128)(2,1)} reshape(bf16[512,1536]{1,0:T(8,128)(2,1)} %broadcast_select_fusion.7) | data formatting | bytes 3145728 | tf_op jit(solution)/shard_map/jit(_take)/select_n | solution.py:57
  73.5 2.7 %fusion.9 = f32[512,512]{1,0:T(8,128)S(1)} fusion(bf16[64,24,512]{2,1,0:T(8,128)(2,1)} %select_n.226, bf16[64,24,512]{2,0,1:T(8,128)(2,1)S(1)} %bitcast.113), kind=kOutput, calls=%fused_computation.16 | convolution fusion | flops 805306368 | bytes 4194304 | tf_op jit(solution)/shard_map/dot_general | solution.py:70
  77.1 1.0 copy.67
  78.0 25.0 %all_to_all.19 = f32[8,520,64]{1,2,0:T(8,128)S(1)} all-to-all(f32[8,520,64]{1,2,0:T(8,128)S(1)} %copy.67), channel_id=1, replica_groups=mesh['elem'=32,'blk'=8] {'blk'}, dimensions={0} | all-to-all | bytes 2129920 | tf_op jit(solution)/shard_map/all_to_all | solution.py:85
  103.4 0.8 reshape.342
  104.3 4.8 %all-to-all-start.2 = ((f32[32,1,1088]{2,1,0:T(1,128)}), f32[32,1,1088]{2,1,0:T(1,128)S(1)}, u32[]{:S(2)}, u32[]{:S(2)}) async-start(f32[32,1,1088]{2,1,0:T(1,128)} %reshape.342), calls=%async_computation.2 | async-start | bytes 294912 | tf_op jit(solution)/shard_map/all_to_all | solution.py:94
  110.4 8.2 %all-to-all-done.2 = f32[32,1,1088]{2,1,0:T(1,128)S(1)} async-done(((f32[32,1,1088]{2,1,0:T(1,128)}), f32[32,1,1088]{2,1,0:T(1,128)S(1)}, u32[]{:S(2)}, u32[]{:S(2)}) %all-to-all-start.2) | async-done | bytes 139296 | tf_op jit(solution)/shard_map/all_to_all | solution.py:94
  119.1 1.0 reduce.6
  (80 shorter events, 10.3 us)
Async XLA Ops:
  5.3 3.2 %copy-start.4 = (s32[1,1,256]{2,1,0:T(1,128)S(1)}, s32[1,1,256]{2,1,0:T(1,128)}, u32[]{:S(2)}) copy-start(s32[1,1,256]{2,1,0:T(1,128)} %param.9) | copy-start | bytes 3076
  12.0 14.1 %copy-start.3 = (s32[8,64]{1,0:T(8,128)S(1)}, s32[8,64]{1,0:T(8,128)}, u32[]{:S(2)}) copy-start(s32[8,64]{1,0:T(8,128)} %param.10) | copy-start | bytes 6148
  12.0 14.6 %copy-start.5 = (bf16[512]{0:T(512)(128)(2,1)S(1)}, bf16[512]{0:T(512)(128)(2,1)}, u32[]{:S(2)}) copy-start(bf16[512]{0:T(512)(128)(2,1)} %param.14) | copy-start | bytes 3076
  14.2 32.9 %all-to-all-start = ((bf16[32,8,1536]{2,1,0:T(8,128)(2,1)}), bf16[32,8,1536]{2,1,0:T(8,128)(2,1)S(1)}, u32[]{:S(2)}, u32[]{:S(2)}) async-start(bf16[32,8,1536]{2,1,0:T(8,128)(2,1)} %bitcast_select_fusion), calls=%async_computation | async-start | bytes 1572864 | tf_op jit(solution)/shard_map/all_to_all | solution.py:55
  26.1 1.6 %copy-start.9 = (s32[32]{0:T(128)S(1)}, s32[32]{0:T(128)}, u32[]{:S(2)}) copy-start(s32[32]{0:T(128)} %param.11) | copy-start | bytes 388
  26.1 2.4 %copy-start.6 = (f32[64]{0:T(128)S(1)}, f32[64]{0:T(128)}, u32[]{:S(2)}) copy-start(f32[64]{0:T(128)} %param.12) | copy-start | bytes 772
  53.5 1.9 %copy-start = (bf16[64,24,512]{2,1,0:T(8,128)(2,1)S(1)}, bf16[64,24,512]{2,1,0:T(8,128)(2,1)}, u32[]{:S(2)}) copy-start(bf16[64,24,512]{2,1,0:T(8,128)(2,1)} %gather.18) | copy-start | bytes 4718596
  55.4 3.6 %copy-start.7 = (f32[64]{0:T(128)S(1)}, f32[64]{0:T(128)}, u32[]{:S(2)}) copy-start(f32[64]{0:T(128)} %param.13) | copy-start | bytes 772
  67.8 4.4 %copy-start.1 = (bf16[64,24,512]{2,1,0:T(8,128)(2,1)S(1)}, bf16[64,24,512]{2,1,0:T(8,128)(2,1)}, u32[]{:S(2)}) copy-start(bf16[64,24,512]{2,1,0:T(8,128)(2,1)} %gather.18) | copy-start | bytes 4718596
  72.1 1.4 %copy-start.2 = (bf16[64,8,3,512]{3,0,2,1:T(8,128)(2,1)S(1)}, bf16[64,8,3,512]{3,0,2,1:T(8,128)(2,1)}, u32[]{:S(2)}) copy-start(bf16[64,8,3,512]{3,0,2,1:T(8,128)(2,1)} %copy.63) | copy-start | bytes 4718596
  103.2 17.6 %copy-start.8 = (f32[64]{0:T(128)S(1)}, f32[64]{0:T(128)}, u32[]{:S(2)}) copy-start(f32[64]{0:T(128)} %param.15) | copy-start | bytes 772
  104.3 14.3 %all-to-all-start.2 = ((f32[32,1,1088]{2,1,0:T(1,128)}), f32[32,1,1088]{2,1,0:T(1,128)S(1)}, u32[]{:S(2)}, u32[]{:S(2)}) async-start(f32[32,1,1088]{2,1,0:T(1,128)} %reshape.342), calls=%async_computation.2 | async-start | bytes 294912 | tf_op jit(solution)/shard_map/all_to_all | solution.py:94
